TPU v7x, 32 devices: a whole 2x2x4 slice. The times are simulated.
32 devices in a mesh: cp: 2 (over y), tp: 4 (over x, core), ep: 4 (over z).
Axes of the slice: x: 2, y: 2, z: 4, core: 2. Of those that a mesh axis runs over, the one named last changes fastest.
Arguments:
- query: bfloat16 [8, 512, 4096], P('ep', 'cp', 'tp'), may hold values from -6 to 6
- keys: bfloat16 [8, 512, 512], P('ep', 'cp', 'tp'), may hold values from -6 to 6
- values: bfloat16 [8, 512, 512], P('ep', 'cp', 'tp'), may hold values from -24 to 24
- segment_ids: int32 [8, 512], P('ep', 'cp'), may hold values from 0 to 3, never falling along the last dimension, each value on 1 to 256 neighbouring positions
- query_norm_gain: float32 [128], replicated, may hold values from 0.25 to 1.75
- key_norm_gain: float32 [128], replicated, may hold values from 0.25 to 1.75
- out_weight: bfloat16 [4096, 2048], P('tp', 'cp'), may hold values from -0.09375 to 0.09375
- residual: bfloat16 [8, 512, 2048], P('ep', 'cp'), may hold values from -3 to 3
- norm_gain: float32 [2048], replicated, may hold values from 0.25 to 1.75
- router_weight: bfloat16 [2048, 16], replicated, may hold values from -0.125 to 0.125
- expert_ids: int32 [8, 512, 8], P('ep', 'cp'), may hold values from 0 to 15, all different within a row; in each aligned block of 64 rows (0 to 63, 64 to 127, ..., all dimensions but the last counted through in order) at most 36 rows name the same one
- expert_gate: bfloat16 [16, 2048, 768], P(('tp', 'ep'), None, 'cp'), may hold values from -0.125 to 0.125
- expert_up: bfloat16 [16, 2048, 768], P(('tp', 'ep'), None, 'cp'), may hold values from -0.125 to 0.125
- expert_down: bfloat16 [16, 2048, 768], P(('tp', 'ep'), None, 'cp'), may hold values from -0.21875 to 0.21875
Outputs:
- layer_out: bfloat16 [8, 512, 2048], P('ep', ('cp', 'tp'))
Inputs may be any that keep to these rules, and one draw needn't show every extreme that they name: `segment_ids`: document numbers never fall along a sequence. `expert_ids`: each token names 8 different experts; in every aligned block of 64 positions of a sequence no expert is named by more than 36 tokens, a bound that some block reaches.
All inputs are finite; a program needn't handle non-finite values.
Results may differ from a plain program's by a relative error of at most 0.007.
Values may be sent and summed in bfloat16 or wider, within the bound.
No kernel may reach another device: no remote copies, remote signals or barrier semaphores. Data moves between devices by JAX's collectives and lax.ppermute only.
A program may use at most 128 MiB of HBM per device.

v0:
```python
import functools
import jax
import jax.numpy as jnp
from jax import lax
from jax.sharding import PartitionSpec as P

HEAD_WIDTH = 128


def root_mean_scale(entries, gain):
    mean_sq = jnp.mean(entries * entries, axis=-1, keepdims=True)
    return entries * lax.rsqrt(mean_sq + 1e-06) * gain


def capacity(share, top_count, experts):
    return min(
        share, max(2, share * top_count // experts + max(1, share * top_count // (8 * experts)))
    )


def slot_numbers(ids, experts):
    flat_ids = ids.reshape(-1)
    table = (flat_ids[:, None] == jnp.arange(experts, dtype=jnp.int32)[None, :]).astype(jnp.int32)
    before = jnp.cumsum(table, axis=0) - table
    return jnp.sum(before * table, axis=1).reshape(ids.shape)


def route(state, ids, norm_gain, router_weight):
    normed = root_mean_scale(state, norm_gain).astype(jnp.bfloat16)
    logits = jnp.dot(normed, router_weight, preferred_element_type=jnp.float32)
    experts = router_weight.shape[1]
    picks = ids[:, :, None] == jnp.arange(experts, dtype=jnp.int32)[None, None, :]
    chosen = jnp.sum(jnp.where(picks, logits[:, None, :], jnp.float32(0.0)), axis=-1)
    raised = jnp.exp(chosen)
    return (normed, raised / jnp.sum(raised, axis=-1, keepdims=True))


def cp_pieces(x, n_cp):
    pieces = [x]
    for shift in range(1, n_cp):
        perm = [(i, (i + shift) % n_cp) for i in range(n_cp)]
        pieces.append(lax.ppermute(x, "cp", perm))
    return pieces


def expert_rows(received, full_gate, full_up, full_down):
    width = received.shape[-1]
    flat_rows = received.reshape(-1, width)
    gate_act = jnp.dot(flat_rows, full_gate[0], preferred_element_type=jnp.float32)
    up_act = jnp.dot(flat_rows, full_up[0], preferred_element_type=jnp.float32)
    hidden_act = (jax.nn.silu(gate_act) * up_act).astype(jnp.bfloat16)
    served = jnp.einsum(
        "rf,df->rd", hidden_act, full_down[0], preferred_element_type=jnp.float32
    ).astype(jnp.bfloat16)
    return served.reshape(received.shape)


def shards(
    query,
    keys,
    values,
    segment_ids,
    query_norm_gain,
    key_norm_gain,
    out_weight,
    residual,
    norm_gain,
    router_weight,
    expert_ids,
    expert_gate,
    expert_up,
    expert_down,
    *,
    n_cp,
    n_tp,
    n_ep
):
    packs = query.shape[0]
    row_count = query.shape[1]
    head_count = query.shape[2] // HEAD_WIDTH
    width = residual.shape[2]
    experts = router_weight.shape[1]
    top_count = expert_ids.shape[2]
    score_scale = HEAD_WIDTH ** (-0.5)
    query_rows_normed = root_mean_scale(
        query.astype(jnp.float32).reshape(packs, row_count, head_count, HEAD_WIDTH), query_norm_gain
    ).astype(jnp.bfloat16)
    key_rows_normed = root_mean_scale(keys.astype(jnp.float32), key_norm_gain).astype(jnp.bfloat16)
    key_value = jnp.concatenate([key_rows_normed, values], axis=-1)
    kv_all = jnp.concatenate(cp_pieces(key_value, n_cp), axis=1)
    doc_all = jnp.concatenate(cp_pieces(segment_ids, n_cp), axis=1)
    key_piece = kv_all[..., :HEAD_WIDTH]
    value_piece = kv_all[..., HEAD_WIDTH:]
    scores = (
        jnp.einsum(
            "pshd,pnd->phsn", query_rows_normed, key_piece, preferred_element_type=jnp.float32
        )
        * score_scale
    )
    same_doc = segment_ids[:, :, None] == doc_all[:, None, :]
    probs = jnp.where(same_doc[:, None], jnp.exp(scores), jnp.float32(0.0))
    denom = jnp.sum(probs, axis=-1)
    probs_b = probs.astype(jnp.bfloat16)
    summed = jnp.einsum("phsn,pnd->pshd", probs_b, value_piece, preferred_element_type=jnp.float32)
    attn = (
        (summed / jnp.transpose(denom, (0, 2, 1))[:, :, :, None])
        .astype(jnp.bfloat16)
        .reshape(packs * row_count, head_count * HEAD_WIDTH)
    )
    share = row_count // n_tp
    tp_index = lax.axis_index("tp")
    ep_index = lax.axis_index("ep")
    cp_index = lax.axis_index("cp")
    cap = capacity(share, top_count, experts)
    attn_pieces = cp_pieces(attn, n_cp)
    received_blocks = []
    for j, piece in enumerate(attn_pieces):
        if j > 0:
            piece, received_blocks[0] = lax.optimization_barrier((piece, received_blocks[0]))
        block = jnp.dot(piece, out_weight, preferred_element_type=jnp.float32).reshape(
            packs, row_count, out_weight.shape[1]
        )
        summed = lax.psum_scatter(block.astype(jnp.bfloat16), "tp", scatter_dimension=1, tiled=True)
        if j > 0:
            summed = lax.ppermute(summed, "cp", [(i, (i - j) % n_cp) for i in range(n_cp)])
        received_blocks.append(summed)
    blocks = jnp.stack(received_blocks, axis=2).astype(jnp.float32)
    source_block = (jnp.arange(n_cp, dtype=jnp.int32) - cp_index) % n_cp
    picks_block = source_block[:, None] == jnp.arange(n_cp, dtype=jnp.int32)[None, :]
    projected = jnp.sum(
        jnp.where(picks_block[None, None, :, :, None], blocks[:, :, None, :, :], jnp.float32(0.0)),
        axis=3,
    ).reshape(packs, share, width)
    first_row = tp_index * share
    state = lax.dynamic_slice_in_dim(residual, first_row, share, 1).astype(jnp.float32) + projected
    local_ids = lax.dynamic_slice_in_dim(expert_ids, first_row, share, 1).reshape(
        packs * share, top_count
    )
    home_rows = packs * share
    normed = root_mean_scale(state.reshape(home_rows, width), norm_gain).astype(jnp.bfloat16)
    attn_pieces, expert_gate, expert_up, expert_down = lax.optimization_barrier(
        (attn_pieces, expert_gate, expert_up, expert_down)
    )
    gate_pieces = cp_pieces(expert_gate, n_cp)
    normed, gate_pieces = lax.optimization_barrier((normed, gate_pieces))
    up_down = jnp.concatenate([expert_up, expert_down], axis=2)
    gate_pieces, up_down = lax.optimization_barrier((gate_pieces, up_down))
    up_down_pieces = cp_pieces(up_down, n_cp)
    lanes = 128
    cap2 = n_ep * cap
    n_slots = n_tp * cap2
    gathered = n_ep * share
    row_iota = jnp.arange(gathered, dtype=jnp.int32)
    earlier = (row_iota[:, None] > row_iota[None, :]).astype(jnp.bfloat16)
    contract = (((0,), (0,)), ((), ()))
    id_lanes = jnp.pad(local_ids.astype(jnp.bfloat16), ((0, 0), (0, lanes - top_count)))
    rows_with_ids = jnp.concatenate([normed, id_lanes], axis=1)
    mixtures = []
    for chunk in range(packs):
        rows = rows_with_ids[chunk * share : (chunk + 1) * share]
        if chunk > 0:
            rows, _ = lax.optimization_barrier((rows, buffer))
        rows_all = lax.all_gather(rows, "ep", axis=0, tiled=True)
        normed_all = rows_all[:, :width]
        ids_all = rows_all[:, width : width + top_count].astype(jnp.int32)
        logits = jnp.dot(normed_all, router_weight, preferred_element_type=jnp.float32)
        picks = ids_all[:, :, None] == jnp.arange(experts, dtype=jnp.int32)[None, None, :]
        raised = jnp.exp(jnp.sum(jnp.where(picks, logits[:, None, :], jnp.float32(0.0)), axis=-1))
        gates_all = raised / jnp.sum(raised, axis=-1, keepdims=True)
        mine = ids_all % n_ep == ep_index
        dest = ids_all // n_ep
        named = jnp.stack(
            [jnp.any(mine & (dest == j), axis=1) for j in range(n_tp)], axis=1
        ).astype(jnp.bfloat16)
        rank = jnp.dot(earlier, named, preferred_element_type=jnp.float32).astype(jnp.int32)
        rank_of = jnp.sum(
            jnp.where(
                dest[:, :, None] == jnp.arange(n_tp, dtype=jnp.int32)[None, None, :],
                rank[:, None, :],
                0,
            ),
            axis=-1,
        )
        target = jnp.where(mine, dest * cap2 + rank_of, jnp.int32(-1)).T
        if chunk == 0:
            full_gate = jnp.concatenate(gate_pieces, axis=2)
        hit = target[:, None, :] == jnp.arange(n_slots, dtype=jnp.int32)[None, :, None]
        select = jnp.any(hit, axis=0).astype(jnp.bfloat16)
        weight = jnp.sum(jnp.where(hit, gates_all.T[:, None, :], jnp.float32(0.0)), axis=0)
        buffer = jnp.dot(select, normed_all, preferred_element_type=jnp.float32).astype(
            jnp.bfloat16
        )
        received = lax.all_to_all(
            buffer.reshape(n_tp, cap2, width), "tp", split_axis=0, concat_axis=0, tiled=True
        )
        if chunk == 0:
            received, up_down_pieces = lax.optimization_barrier((received, up_down_pieces))
            units = expert_up.shape[2]
            full_up = jnp.concatenate([p[:, :, :units] for p in up_down_pieces], axis=2)
            full_down = jnp.concatenate([p[:, :, units:] for p in up_down_pieces], axis=2)
        served = expert_rows(received, full_gate, full_up, full_down)
        back = lax.all_to_all(served, "tp", split_axis=0, concat_axis=0, tiled=True).reshape(
            n_slots, width
        )
        weight_hi = weight.astype(jnp.bfloat16)
        weight_lo = (weight - weight_hi.astype(jnp.float32)).astype(jnp.bfloat16)
        partial = lax.dot_general(
            weight_hi, back, contract, preferred_element_type=jnp.float32
        ) + lax.dot_general(weight_lo, back, contract, preferred_element_type=jnp.float32)
        mixtures.append(
            lax.psum_scatter(
                partial.astype(jnp.bfloat16).reshape(n_ep, share, width),
                "ep",
                scatter_dimension=0,
                tiled=True,
            )
        )
    mixture = jnp.concatenate(mixtures, axis=0).astype(jnp.float32)
    layer_out = (state + mixture).astype(jnp.bfloat16)
    return layer_out


def solution(mesh):
    body = functools.partial(
        shards, n_cp=mesh.shape["cp"], n_tp=mesh.shape["tp"], n_ep=mesh.shape["ep"]
    )
    return jax.shard_map(
        body,
        mesh=mesh,
        in_specs=(
            P("ep", "cp", "tp"),
            P("ep", "cp", "tp"),
            P("ep", "cp", "tp"),
            P("ep", "cp"),
            P(),
            P(),
            P("tp", "cp"),
            P("ep", "cp", None),
            P(),
            P(),
            P("ep", "cp", None),
            P(("tp", "ep"), None, "cp"),
            P(("tp", "ep"), None, "cp"),
            P(("tp", "ep"), None, "cp"),
        ),
        out_specs=P("ep", ("cp", "tp"), None),
        check_vma=False,
    )
```

profile of v0, /device:TPU:0, one launch (start us, length us, event | category | flops | bytes accessed | tf_op | source)
XLA Modules:
  0.0 310.7 jit_solution(364503522960644901)
XLA Ops:
  6.5 3.0 collective-permute-start.1
  16.5 1.9 fusion.13
  20.4 2.2 fusion
  25.3 2.3 fusion.23
  27.6 1.7 copy.87
  30.1 23.3 %collective-permute-done.2 = bf16[512,1024]{1,0:T(8,128)(2,1)S(1)} collective-permute-done((bf16[512,1024]{1,0:T(8,128)(2,1)S(1)}, bf16[512,1024]{1,0:T(8,128)(2,1)S(1)}, u32[]{:S(2)}, u32[]{:S(2)}) %collective-permute-start.2) | collective-permute-done | bytes 1048608 | tf_op jit(solution)/shard_map/ppermute | solution.py:42
  53.4 2.3 convolution_convert_fusion.4
  56.9 24.5 %reduce-scatter.7.cloned.1.call-done = bf16[2,64,1024]{2,1,0:T(8,128)(2,1)} async-done(((bf16[2,256,1024]{2,1,0:T(8,128)(2,1)}), bf16[2,64,1024]{2,1,0:T(8,128)(2,1)}) %reduce-scatter.7.cloned.1.call-update) | async-done | bytes 262160 | tf_op jit(solution)/shard_map/reduce_scatter | solution.py:123
  83.0 14.3 %collective-permute-done.3 = bf16[2,64,1024]{2,1,0:T(8,128)(2,1)S(1)} collective-permute-done((bf16[2,64,1024]{2,1,0:T(8,128)(2,1)}, bf16[2,64,1024]{2,1,0:T(8,128)(2,1)S(1)}, u32[]{:S(2)}, u32[]{:S(2)}) %collective-permute-start.3) | collective-permute-done | bytes 262176 | tf_op jit(solution)/shard_map/ppermute | solution.py:125
  100.3 3.8 %pad_maximum_fusion = bf16[1,2048,768]{2,1,0:T(8,128)(2,1)} fusion(bf16[1,2048,384]{2,1,0:T(8,128)(2,1)} %param.27, bf16[1,2048,384]{2,1,0:T(8,128)(2,1)} %param.26), kind=kLoop, calls=%fused_computation.13 | loop fusion | flops 6291456 | bytes 6291456 | tf_op jit(solution)/shard_map/concatenate | solution.py:146
  105.6 23.9 %all-gather.3.cloned.1.call-done = bf16[256,2176]{1,0:T(8,128)(2,1)} async-done(((bf16[64,2176]{1,0:T(8,128)(2,1)}), bf16[256,2176]{1,0:T(8,128)(2,1)}) %all-gather.3.cloned.1.call-update) | async-done | bytes 1114128 | tf_op jit(solution)/shard_map/all_gather | solution.py:163
  131.5 3.4 %convolution_convert_fusion.3 = bf16[576,2048]{1,0:T(8,128)(2,1)} fusion(pred[576,256]{1,0:T(8,128)(4,1)S(1)} %fusion.3, bf16[256,2176]{1,0:T(8,128)(2,1)} %all-gather.3.cloned.1.call-done), kind=kOutput, calls=%fused_computation.20 | convolution fusion | flops 605159424 | bytes 3555328 | tf_op jit(solution)/shard_map/dot_general | solution.py:190
  135.0 4.8 %all-to-all-start = ((bf16[4,144,2048]{2,1,0:T(8,128)(2,1)}), bf16[4,144,2048]{2,1,0:T(8,128)(2,1)}, u32[]{:S(2)}, u32[]{:S(2)}) async-start(bf16[4,144,2048]{2,1,0:T(8,128)(2,1)} %bitcast.119), calls=%async_computation.2 | async-start | bytes 4718592 | tf_op jit(solution)/shard_map/all_to_all | solution.py:193
  140.3 23.3 %all-gather.5.cloned.1.call-done = bf16[256,2176]{1,0:T(8,128)(2,1)} async-done(((bf16[64,2176]{1,0:T(8,128)(2,1)}), bf16[256,2176]{1,0:T(8,128)(2,1)}) %all-gather.5.cloned.1.call-update) | async-done | bytes 1114128 | tf_op jit(solution)/shard_map/all_gather | solution.py:163
  165.6 3.4 %convolution_convert_fusion.2 = bf16[576,2048]{1,0:T(8,128)(2,1)} fusion(pred[576,256]{1,0:T(8,128)(4,1)S(1)} %fusion.2, bf16[256,2176]{1,0:T(8,128)(2,1)} %all-gather.5.cloned.1.call-done), kind=kOutput, calls=%fused_computation.19 | convolution fusion | flops 605159424 | bytes 3555328 | tf_op jit(solution)/shard_map/dot_general | solution.py:190
  169.0 4.6 %all-to-all-start.2 = ((bf16[4,144,2048]{2,1,0:T(8,128)(2,1)}), bf16[4,144,2048]{2,1,0:T(8,128)(2,1)}, u32[]{:S(2)}, u32[]{:S(2)}) async-start(bf16[4,144,2048]{2,1,0:T(8,128)(2,1)} %bitcast.120), calls=%async_computation.5 | async-start | bytes 4718592 | tf_op jit(solution)/shard_map/all_to_all | solution.py:193
  173.7 5.4 %fusion.20 = f32[576,768]{1,0:T(8,128)} fusion(bf16[576,2048]{1,0:T(8,128)(2,1)} %bitcast.16, bf16[1,2048,384]{2,1,0:T(8,128)(2,1)} %collective-permute-done.4, bf16[1,2048,384]{2,1,0:T(8,128)(2,1)S(1)} %copy-done.13), kind=kOutput, calls=%fused_computation.38 | convolution fusion | flops 1818230784 | bytes 7274496 | tf_op jit(solution)/shard_map/dot_general | solution.py:49
  179.1 5.2 %fusion.82 = (bf16[1,2048,384]{2,1,0:T(8,128)(2,1)S(1)}, bf16[1,2048,384]{2,1,0:T(8,128)(2,1)}, bf16[1,2048,384]{2,1,0:T(8,128)(2,1)}, bf16[1,2048,384]{2,1,0:T(8,128)(2,1)}) fusion(bf16[1,2048,768]{2,1,0:T(8,128)(2,1)} %pad_maximum_fusion, bf16[1,2048,768]{2,1,0:T(8,128)(2,1)} %collective-permute-done.5), kind=kLoop, calls=%fused_computation.157 | loop fusion | bytes 12582912 | tf_op jit(solution)/shard_map/slice | solution.py:199
  184.3 9.4 %convolution_convert_fusion.1 = bf16[576,2048]{1,0:T(8,128)(2,1)} fusion(bf16[1,2048,384]{2,1,0:T(8,128)(2,1)} %get-tuple-element.57, bf16[1,2048,384]{2,1,0:T(8,128)(2,1)} %get-tuple-element.50, f32[576,768]{1,0:T(8,128)} %fusion.20, bf16[576,2048]{1,0:T(8,128)(2,1)} %bitcast.16, bf16[1,2048,384]{2,1,0:T(8,128)(2,1)} %get-tuple-element.58, ...), kind=kOutput, calls=%fused_computation.18 | convolution fusion | flops 3640295424 | bytes 12779520 | tf_op jit(solution)/shard_map/rf,df->rd/dot_general | solution.py:52
  193.6 8.6 %all-to-all-done.2 = bf16[4,144,2048]{2,1,0:T(8,128)(2,1)} async-done(((bf16[4,144,2048]{2,1,0:T(8,128)(2,1)}), bf16[4,144,2048]{2,1,0:T(8,128)(2,1)}, u32[]{:S(2)}, u32[]{:S(2)}) %all-to-all-start.2) | async-done | bytes 2359328 | tf_op jit(solution)/shard_map/all_to_all | solution.py:193
  202.2 4.7 %all-to-all-start.1 = ((bf16[4,144,2048]{2,1,0:T(8,128)(2,1)}), bf16[4,144,2048]{2,1,0:T(8,128)(2,1)}, u32[]{:S(2)}, u32[]{:S(2)}) async-start(bf16[4,144,2048]{2,1,0:T(8,128)(2,1)} %bitcast.128), calls=%async_computation.3 | async-start | bytes 4718592 | tf_op jit(solution)/shard_map/all_to_all | solution.py:202
  208.4 5.8 %fusion.19 = f32[576,768]{1,0:T(8,128)} fusion(bf16[576,2048]{1,0:T(8,128)(2,1)} %bitcast.26, bf16[1,2048,384]{2,1,0:T(8,128)(2,1)} %collective-permute-done.4, bf16[1,2048,384]{2,1,0:T(8,128)(2,1)} %param.25), kind=kOutput, calls=%fused_computation.37 | convolution fusion | flops 1818230784 | bytes 7274496 | tf_op jit(solution)/shard_map/dot_general | solution.py:49
  214.2 9.4 %convolution_convert_fusion = bf16[576,2048]{1,0:T(8,128)(2,1)} fusion(bf16[1,2048,384]{2,1,0:T(8,128)(2,1)} %get-tuple-element.57, bf16[1,2048,384]{2,1,0:T(8,128)(2,1)} %get-tuple-element.50, f32[576,768]{1,0:T(8,128)} %fusion.19, bf16[576,2048]{1,0:T(8,128)(2,1)} %bitcast.26, bf16[1,2048,384]{2,1,0:T(8,128)(2,1)} %get-tuple-element.58, ...), kind=kOutput, calls=%fused_computation.17 | convolution fusion | flops 3640295424 | bytes 12779520 | tf_op jit(solution)/shard_map/rf,df->rd/dot_general | solution.py:52
  223.7 11.6 %all-to-all-done.1 = bf16[4,144,2048]{2,1,0:T(8,128)(2,1)} async-done(((bf16[4,144,2048]{2,1,0:T(8,128)(2,1)}), bf16[4,144,2048]{2,1,0:T(8,128)(2,1)}, u32[]{:S(2)}, u32[]{:S(2)}) %all-to-all-start.1) | async-done | bytes 2359328 | tf_op jit(solution)/shard_map/all_to_all | solution.py:202
  235.3 4.5 %all-to-all-start.3 = ((bf16[4,144,2048]{2,1,0:T(8,128)(2,1)}), bf16[4,144,2048]{2,1,0:T(8,128)(2,1)}, u32[]{:S(2)}, u32[]{:S(2)}) async-start(bf16[4,144,2048]{2,1,0:T(8,128)(2,1)} %bitcast.127), calls=%async_computation.6 | async-start | bytes 4718592 | tf_op jit(solution)/shard_map/all_to_all | solution.py:202
  239.9 2.9 fusion.45
  242.8 3.7 %fusion.9 = bf16[256,2048]{1,0:T(8,128)(2,1)} fusion(f32[256,2048]{1,0:T(8,128)S(1)} %fusion.45, bf16[576,2048]{1,0:T(8,128)(2,1)} %bitcast.21, f32[576,256]{1,0:T(8,128)S(1)} %copy-done.3), kind=kOutput, calls=%fused_computation.23 | convolution fusion | flops 605618176 | bytes 6094848 | tf_op jit(solution)/shard_map/dot_general | solution.py:209
  248.9 19.5 %all-to-all-done.3 = bf16[4,144,2048]{2,1,0:T(8,128)(2,1)} async-done(((bf16[4,144,2048]{2,1,0:T(8,128)(2,1)}), bf16[4,144,2048]{2,1,0:T(8,128)(2,1)}, u32[]{:S(2)}, u32[]{:S(2)}) %all-to-all-start.3) | async-done | bytes 2359328 | tf_op jit(solution)/shard_map/all_to_all | solution.py:202
  268.4 2.7 fusion.42
  271.1 4.2 %fusion.10 = bf16[256,2048]{1,0:T(8,128)(2,1)} fusion(f32[256,2048]{1,0:T(8,128)S(1)} %fusion.42, bf16[576,2048]{1,0:T(8,128)(2,1)} %bitcast.28, f32[576,256]{1,0:T(8,128)} %copy-done.4), kind=kOutput, calls=%fused_computation.24 | convolution fusion | flops 605618176 | bytes 6094848 | tf_op jit(solution)/shard_map/dot_general | solution.py:209
  275.4 26.5 %reduce-scatter.11.cloned.1.call-done = bf16[1,64,2048]{2,1,0:T(8,128)(2,1)} async-done(((bf16[4,64,2048]{2,1,0:T(8,128)(2,1)}), bf16[1,64,2048]{2,1,0:T(8,128)(2,1)}) %reduce-scatter.11.cloned.1.call-update) | async-done | bytes 262160 | tf_op jit(solution)/shard_map/reduce_scatter | solution.py:211
  301.9 1.9 add_convert_fusion
  (114 shorter events, 27.9 us)
Async XLA Ops:
  6.5 18.7 %copy-start = (bf16[1024,1024]{1,0:T(8,128)(2,1)S(1)}, bf16[1024,1024]{1,0:T(8,128)(2,1)}, u32[]{:S(2)}) copy-start(bf16[1024,1024]{1,0:T(8,128)(2,1)} %param.20) | copy-start | bytes 6291460
  6.5 46.8 %reduce-scatter.5.cloned.1.call-start = ((), (), s32[]{:S(2)}) async-start(), calls=%async_computation.8 | async-start | bytes 1310720 | tf_op jit(solution)/shard_map/reduce_scatter | solution.py:123
  6.5 12.0 %collective-permute-start.1 = (s32[2,256]{1,0:T(2,128)}, s32[2,256]{1,0:T(2,128)S(1)}, u32[]{:S(2)}, u32[]{:S(2)}) collective-permute-start(s32[2,256]{1,0:T(2,128)} %param.17), channel_id=1, source_target_pairs={{0,16},{16,0},{1,17},{17,1},{2,18},{18,2},{3,19},{19,3},{4,20},{20... | collective-permute-start | bytes 6152 | tf_op jit(solution)/shard_map/ppermute | solution.py:42
  12.6 7.8 %collective-permute-start = (bf16[2,256,256]{2,1,0:T(8,128)(2,1)S(1)}, bf16[2,256,256]{2,1,0:T(8,128)(2,1)S(1)}, u32[]{:S(2)}, u32[]{:S(2)}) collective-permute-start(bf16[2,256,256]{2,1,0:T(8,128)(2,1)S(1)} %pad_maximum_fusion.2), channel_id=1, source_target_pairs={{0,16},{16,0},{1,17},{17,1},{2,18},{18,2},{3,19},{19,3},{4,20},{20... | collective-permute-start | bytes 786440 | tf_op jit(solution)/shard_map/ppermute | solution.py:42
  12.8 3.8 %copy-start.12 = (f32[128]{0:T(128)S(1)}, f32[128]{0:T(128)}, u32[]{:S(2)}) copy-start(f32[128]{0:T(128)} %param.18) | copy-start | bytes 1540
  14.3 1.4 copy-start.2
  16.3 2.2 copy-start.10
  16.3 4.1 %copy-start.7 = (bf16[2,256,128]{2,1,0:T(8,128)(2,1)S(1)}, bf16[2,256,128]{2,1,0:T(8,128)(2,1)}, u32[]{:S(2)}) copy-start(bf16[2,256,128]{2,1,0:T(8,128)(2,1)} %param.16) | copy-start | bytes 393220
  24.3 1.0 copy-start.5
  27.5 53.8 %reduce-scatter.7.cloned.1.call-start = ((), (), s32[]{:S(2)}) async-start(), calls=%async_computation.9 | async-start | bytes 1310720 | tf_op jit(solution)/shard_map/reduce_scatter | solution.py:123
  29.6 27.2 %copy-start.11 = (s32[2,256,8]{1,2,0:T(8,128)S(1)}, s32[2,256,8]{1,2,0:T(8,128)}, u32[]{:S(2)}) copy-start(s32[2,256,8]{1,2,0:T(8,128)} %param.24) | copy-start | bytes 49156
  29.6 23.8 %collective-permute-start.2 = (bf16[512,1024]{1,0:T(8,128)(2,1)S(1)}, bf16[512,1024]{1,0:T(8,128)(2,1)S(1)}, u32[]{:S(2)}, u32[]{:S(2)}) collective-permute-start(bf16[512,1024]{1,0:T(8,128)(2,1)S(1)} %bitcast.131), channel_id=1, source_target_pairs={{0,16},{16,0},{1,17},{17,1},{2,18},{18,2},{3,19},{19,3},{4,20},{20... | collective-permute-start | bytes 3145736 | tf_op jit(solution)/shard_map/ppermute | solution.py:42
  53.4 43.9 %copy-start.8 = (bf16[2,64,1024]{2,1,0:T(8,128)(2,1)S(1)}, bf16[2,64,1024]{2,1,0:T(8,128)(2,1)}, u32[]{:S(2)}) copy-start(bf16[2,64,1024]{2,1,0:T(8,128)(2,1)} %reduce-scatter.5.cloned.1.call-done) | copy-start | bytes 786436
  55.7 73.8 %all-gather.3.cloned.1.call-start = ((), (), s32[]{:S(2)}) async-start(), calls=%async_computation.10 | async-start | bytes 1392640 | tf_op jit(solution)/shard_map/all_gather | solution.py:163
  55.7 43.6 %collective-permute-start.4 = (bf16[1,2048,384]{2,1,0:T(8,128)(2,1)}, bf16[1,2048,384]{2,1,0:T(8,128)(2,1)}, u32[]{:S(2)}, u32[]{:S(2)}) collective-permute-start(bf16[1,2048,384]{2,1,0:T(8,128)(2,1)} %param.25), channel_id=1, source_target_pairs={{0,16},{16,0},{1,17},{17,1},{2,18},{18,2},{3,19},{19,3},{4,20},{20... | collective-permute-start | bytes 4718600 | tf_op jit(solution)/shard_map/ppermute | solution.py:42
  81.3 16.0 %collective-permute-start.3 = (bf16[2,64,1024]{2,1,0:T(8,128)(2,1)}, bf16[2,64,1024]{2,1,0:T(8,128)(2,1)S(1)}, u32[]{:S(2)}, u32[]{:S(2)}) collective-permute-start(bf16[2,64,1024]{2,1,0:T(8,128)(2,1)} %reduce-scatter.7.cloned.1.call-done), channel_id=1, source_target_pairs={{0,16},{16,0},{1,17},{17,1},{2,18},{18,2},{3,19},{19,3},{4,20},{20... | collective-permute-start | bytes 786440 | tf_op jit(solution)/shard_map/ppermute | solution.py:125
  97.7 1.5 copy-start.9
  100.3 63.3 %all-gather.5.cloned.1.call-start = ((), (), s32[]{:S(2)}) async-start(), calls=%async_computation.12 | async-start | bytes 1392640 | tf_op jit(solution)/shard_map/all_gather | solution.py:163
  104.1 69.6 %collective-permute-start.5 = (bf16[1,2048,768]{2,1,0:T(8,128)(2,1)}, bf16[1,2048,768]{2,1,0:T(8,128)(2,1)}, u32[]{:S(2)}, u32[]{:S(2)}) collective-permute-start(bf16[1,2048,768]{2,1,0:T(8,128)(2,1)} %pad_maximum_fusion), channel_id=1, source_target_pairs={{0,16},{16,0},{1,17},{17,1},{2,18},{18,2},{3,19},{19,3},{4,20},{20... | collective-permute-start | bytes 9437192 | tf_op jit(solution)/shard_map/ppermute | solution.py:42
  134.9 4.9 %copy-start.6 = (bf16[256,2176]{1,0:T(8,128)(2,1)S(1)}, bf16[256,2176]{1,0:T(8,128)(2,1)}, u32[]{:S(2)}) copy-start(bf16[256,2176]{1,0:T(8,128)(2,1)} %all-gather.3.cloned.1.call-done) | copy-start | bytes 3342340
  134.9 4.9 %copy-start.14 = (bf16[2048,16]{0,1:T(8,128)(2,1)S(1)}, bf16[2048,16]{0,1:T(8,128)(2,1)}, u32[]{:S(2)}) copy-start(bf16[2048,16]{0,1:T(8,128)(2,1)} %param.23) | copy-start | bytes 196612
  135.0 34.1 %all-to-all-start = ((bf16[4,144,2048]{2,1,0:T(8,128)(2,1)}), bf16[4,144,2048]{2,1,0:T(8,128)(2,1)}, u32[]{:S(2)}, u32[]{:S(2)}) async-start(bf16[4,144,2048]{2,1,0:T(8,128)(2,1)} %bitcast.119), calls=%async_computation.2 | async-start | bytes 4718592 | tf_op jit(solution)/shard_map/all_to_all | solution.py:193
  169.0 4.7 %copy-start.13 = (bf16[1,2048,384]{2,1,0:T(8,128)(2,1)S(1)}, bf16[1,2048,384]{2,1,0:T(8,128)(2,1)}, u32[]{:S(2)}) copy-start(bf16[1,2048,384]{2,1,0:T(8,128)(2,1)} %param.25) | copy-start | bytes 4718596
  169.0 33.2 %all-to-all-start.2 = ((bf16[4,144,2048]{2,1,0:T(8,128)(2,1)}), bf16[4,144,2048]{2,1,0:T(8,128)(2,1)}, u32[]{:S(2)}, u32[]{:S(2)}) async-start(bf16[4,144,2048]{2,1,0:T(8,128)(2,1)} %bitcast.120), calls=%async_computation.5 | async-start | bytes 4718592 | tf_op jit(solution)/shard_map/all_to_all | solution.py:193
  202.2 33.1 %all-to-all-start.1 = ((bf16[4,144,2048]{2,1,0:T(8,128)(2,1)}), bf16[4,144,2048]{2,1,0:T(8,128)(2,1)}, u32[]{:S(2)}, u32[]{:S(2)}) async-start(bf16[4,144,2048]{2,1,0:T(8,128)(2,1)} %bitcast.128), calls=%async_computation.3 | async-start | bytes 4718592 | tf_op jit(solution)/shard_map/all_to_all | solution.py:202
  235.3 33.1 %all-to-all-start.3 = ((bf16[4,144,2048]{2,1,0:T(8,128)(2,1)}), bf16[4,144,2048]{2,1,0:T(8,128)(2,1)}, u32[]{:S(2)}, u32[]{:S(2)}) async-start(bf16[4,144,2048]{2,1,0:T(8,128)(2,1)} %bitcast.127), calls=%async_computation.6 | async-start | bytes 4718592 | tf_op jit(solution)/shard_map/all_to_all | solution.py:202
  239.8 35.5 %reduce-scatter.9.cloned.1.call-start = ((), (), s32[]{:S(2)}) async-start(), calls=%async_computation.11 | async-start | bytes 1310720 | tf_op jit(solution)/shard_map/reduce_scatter | solution.py:211
  239.9 2.9 copy-start.3
  246.6 55.3 %reduce-scatter.11.cloned.1.call-start = ((), (), s32[]{:S(2)}) async-start(), calls=%async_computation.13 | async-start | bytes 1310720 | tf_op jit(solution)/shard_map/reduce_scatter | solution.py:211
  248.9 19.5 %copy-start.4 = (f32[576,256]{1,0:T(8,128)}, f32[576,256]{1,0:T(8,128)S(1)}, u32[]{:S(2)}) copy-start(f32[576,256]{1,0:T(8,128)S(1)} %select_reduce_fusion) | copy-start | bytes 1769476
  271.1 32.7 %copy-start.1 = (bf16[1024,1024]{1,0:T(8,128)(2,1)S(1)}, bf16[1024,1024]{1,0:T(8,128)(2,1)}, u32[]{:S(2)}) copy-start(bf16[1024,1024]{1,0:T(8,128)(2,1)} %param.20) | copy-start | bytes 6291460
Sparse Core Ops, SparseCore 0:
  27.7 25.2 reduce-scatter.4
  55.8 25.5 reduce-scatter.6
  100.4 29.0 all-gather.2
  135.1 28.4 all-gather.4
  246.7 27.0 reduce-scatter.8
  276.0 25.7 reduce-scatter.10
where the time goes:
time: 312 us; the launch traced here: 311 us
  waiting for transfers between devices  177 us (57%)
  matrix products  60.9 us (20%)
  starting transfers between devices  26.6 us (9%)
  other arithmetic  17.6 us (6%)
  local copies, waits for them, and re-layouts  14.3 us (5%)
  between operations  14 us (4%)
    all_gather x2, waiting for transfers between devices, shards(): rows_all = lax.all_gather(rows, 'ep', axis=0, tiled=True)  47.2 us
    all_to_all x2, waiting for transfers between devices, shards(): lax.all_to_all(served, 'tp', split_axis=0, concat_axis=0, tiled=True)  31.1 us
    reduce_scatter x2, waiting for transfers between devices, shards(): lax.psum_scatter(partial.astype(jnp.bfloat16).reshape(n_ep, share, width)...  26.5 us
    ppermute x5, waiting for transfers between devices, cp_pieces(): pieces.append(lax.ppermute(x, 'cp', perm))  24.9 us
    reduce_scatter x2, waiting for transfers between devices, shards(): lax.psum_scatter(block.astype(jnp.bfloat16), 'tp', scatter_dimension=1, t...  24.5 us
    dot_general x2, matrix products, expert_rows(): jnp.einsum('rf,df->rd', hidden_act, full_down[0], preferred_element_type=...  18.8 us
    ppermute x1, waiting for transfers between devices, shards(): lax.ppermute(summed, 'cp', [(i, (i - j) % n_cp) for i in range(n_cp)])  14.3 us
    dot_general x2, matrix products, expert_rows(): jnp.dot(flat_rows, full_gate[0], preferred_element_type=jnp.float32)  11.2 us
  transfers between devices with their start and end apart: 16, of which 10 were waited for; matrix products, arithmetic and copies ran while one was open for 25% of the time, Pallas kernels for 0%

commit v1 on v0

--- a/solution.py
+++ b/solution.py
@@ -5,6 +5,12 @@
 from jax.sharding import PartitionSpec as P
 
 HEAD_WIDTH = 128
+
+
+def in_order(blocks, dim):
+    blocks = jnp.moveaxis(blocks, 0, dim)
+    dims = blocks.shape
+    return blocks.reshape(*dims[:dim], dims[dim] * dims[dim + 1], *dims[dim + 2 :])
 
 
 def root_mean_scale(entries, gain):
@@ -160,7 +166,19 @@
         rows = rows_with_ids[chunk * share : (chunk + 1) * share]
         if chunk > 0:
             rows, _ = lax.optimization_barrier((rows, buffer))
-        rows_all = lax.all_gather(rows, "ep", axis=0, tiled=True)
+        count = lax.axis_size("ep")
+        pairs = [(i_2, (i_2 + 1) % count) for i_2 in range(count)]
+        back_2 = [(b, a) for a, b in pairs]
+        lower, upper = ([], [])
+        for step in range(count - 1):
+            if step % 2 == 0:
+                lower.append(lax.ppermute(lower[-1] if lower else rows, "ep", pairs))
+            else:
+                upper.append(lax.ppermute(upper[-1] if upper else rows, "ep", back_2))
+        parts = jnp.stack([*lower[::-1], rows, *upper])
+        offset = lax.axis_index("ep") - len(lower)
+        parts = parts[(jnp.arange(count) - offset) % count]
+        rows_all = in_order(parts, 0)
         normed_all = rows_all[:, :width]
         ids_all = rows_all[:, width : width + top_count].astype(jnp.int32)
         logits = jnp.dot(normed_all, router_weight, preferred_element_type=jnp.float32)

time: 312 us -> 358 us (1.15)
  waiting for transfers between devices: 177 us -> 210 us
  starting transfers between devices: 26.6 us -> 36.5 us
    all_gather x2 -> x0, waiting for transfers between devices: 47.2 us -> none  [shards(): rows_all = lax.all_gather(rows, 'ep', axis=0, tiled=True)]
    all_to_all x2, waiting for transfers between devices: 8.64 us -> 45.3 us  [shards(): lax.all_to_all(buffer.reshape(n_tp, cap2, width), 'tp', split_axis=0, con...]
    ppermute x0 -> x6, waiting for transfers between devices: none -> 31.4 us  [the longest x4 26.4 us: shards(): lower.append(lax.ppermute(lower[-1] if lower else rows, 'ep', pairs))]
    ppermute x5, waiting for transfers between devices: 24.9 us -> 37.8 us  [cp_pieces(): pieces.append(lax.ppermute(x, 'cp', perm))]
    ppermute x0 -> x6, starting transfers between devices: none -> 9.38 us  [the longest x2 6.15 us: shards(): upper.append(lax.ppermute(upper[-1] if upper else rows, 'ep', back_2))]
    gather x0 -> x2, local copies, waits for them, and re-layouts: none -> 4.86 us  [shards(): parts = parts[(jnp.arange(count) - offset) % count]]
  transfers between devices with their start and end apart: 16 -> 20, of which waited for: 10 -> 16; matrix products, arithmetic and copies ran while one was open for 25% -> 15% of each run, Pallas kernels for 0% -> 0%
where the time goes in v1:
time: 358 us; the launch traced here: 357 us
  waiting for transfers between devices  210 us (59%)
  matrix products  60.2 us (17%)
  starting transfers between devices  36.5 us (10%)
  other arithmetic  19.5 us (5%)
  local copies, waits for them, and re-layouts  17.4 us (5%)
  between operations  13.7 us (4%)
    all_to_all x2, waiting for transfers between devices, shards(): lax.all_to_all(buffer.reshape(n_tp, cap2, width), 'tp', split_axis=0, con...  45.3 us
    ppermute x5, waiting for transfers between devices, cp_pieces(): pieces.append(lax.ppermute(x, 'cp', perm))  37.8 us
    all_to_all x2, waiting for transfers between devices, shards(): lax.all_to_all(served, 'tp', split_axis=0, concat_axis=0, tiled=True)  31.2 us
    ppermute x4, waiting for transfers between devices, shards(): lower.append(lax.ppermute(lower[-1] if lower else rows, 'ep', pairs))  26.4 us
    reduce_scatter x2, waiting for transfers between devices, shards(): lax.psum_scatter(partial.astype(jnp.bfloat16).reshape(n_ep, share, width)...  25.4 us
    reduce_scatter x2, waiting for transfers between devices, shards(): lax.psum_scatter(block.astype(jnp.bfloat16), 'tp', scatter_dimension=1, t...  24.5 us
    dot_general x2, matrix products, expert_rows(): jnp.einsum('rf,df->rd', hidden_act, full_down[0], preferred_element_type=...  18.8 us
    ppermute x1, waiting for transfers between devices, shards(): lax.ppermute(summed, 'cp', [(i, (i - j) % n_cp) for i in range(n_cp)])  14.3 us
  transfers between devices with their start and end apart: 20, of which 16 were waited for; matrix products, arithmetic and copies ran while one was open for 15% of the time, Pallas kernels for 0%

profile of v1, /device:TPU:0, one launch (start us, length us, event | category | flops | bytes accessed | tf_op | source)
XLA Modules:
  0.0 357.2 jit_solution(12870868675964018986)
XLA Ops:
  6.5 3.0 collective-permute-start.1
  30.2 23.3 %collective-permute-done.2 = bf16[512,1024]{1,0:T(8,128)(2,1)S(1)} collective-permute-done((bf16[512,1024]{1,0:T(8,128)(2,1)S(1)}, bf16[512,1024]{1,0:T(8,128)(2,1)S(1)}, u32[]{:S(2)}, u32[]{:S(2)}) %collective-permute-start.2) | collective-permute-done | bytes 1048608 | tf_op jit(solution)/shard_map/ppermute | solution.py:48
  56.9 24.5 %reduce-scatter.7.cloned.1.call-done = bf16[2,64,1024]{2,1,0:T(8,128)(2,1)} async-done(((bf16[2,256,1024]{2,1,0:T(8,128)(2,1)}), bf16[2,64,1024]{2,1,0:T(8,128)(2,1)}) %reduce-scatter.7.cloned.1.call-update) | async-done | bytes 262160 | tf_op jit(solution)/shard_map/reduce_scatter | solution.py:129
  83.0 14.3 %collective-permute-done.3 = bf16[2,64,1024]{2,1,0:T(8,128)(2,1)S(1)} collective-permute-done((bf16[2,64,1024]{2,1,0:T(8,128)(2,1)}, bf16[2,64,1024]{2,1,0:T(8,128)(2,1)S(1)}, u32[]{:S(2)}, u32[]{:S(2)}) %collective-permute-start.3) | collective-permute-done | bytes 262176 | tf_op jit(solution)/shard_map/ppermute | solution.py:131
  103.4 7.6 %collective-permute-done.5 = bf16[64,2176]{1,0:T(8,128)(2,1)S(1)} collective-permute-done((bf16[64,2176]{1,0:T(8,128)(2,1)S(1)}, bf16[64,2176]{1,0:T(8,128)(2,1)S(1)}, u32[]{:S(2)}, u32[]{:S(2)}) %collective-permute-start.5) | collective-permute-done | bytes 278560 | tf_op jit(solution)/shard_map/ppermute | solution.py:175
  112.1 3.3 collective-permute-done.7
  115.5 4.9 %collective-permute-done.6 = bf16[64,2176]{1,0:T(8,128)(2,1)S(1)} collective-permute-done((bf16[64,2176]{1,0:T(8,128)(2,1)S(1)}, bf16[64,2176]{1,0:T(8,128)(2,1)S(1)}, u32[]{:S(2)}, u32[]{:S(2)}) %collective-permute-start.6) | collective-permute-done | bytes 278560 | tf_op jit(solution)/shard_map/ppermute | solution.py:175
  126.9 3.8 %collective-permute-start.11 = (bf16[64,2176]{1,0:T(8,128)(2,1)S(1)}, bf16[64,2176]{1,0:T(8,128)(2,1)S(1)}, u32[]{:S(2)}, u32[]{:S(2)}) collective-permute-start(bf16[64,2176]{1,0:T(8,128)(2,1)S(1)} %get-tuple-element.34), channel_id=1, source_target_pairs={{1,0},{2,1},{3,2},{0,3},{5,4},{6,5},{7,6},{4,7},{9,8},{10,9},{11,1... | collective-permute-start | bytes 835592 | tf_op jit(solution)/shard_map/ppermute | solution.py:177
  130.7 7.7 %collective-permute-done.9 = bf16[64,2176]{1,0:T(8,128)(2,1)S(1)} collective-permute-done((bf16[64,2176]{1,0:T(8,128)(2,1)S(1)}, bf16[64,2176]{1,0:T(8,128)(2,1)S(1)}, u32[]{:S(2)}, u32[]{:S(2)}) %collective-permute-start.9) | collective-permute-done | bytes 278560 | tf_op jit(solution)/shard_map/ppermute | solution.py:175
  140.6 6.3 %collective-permute-done.10 = bf16[64,2176]{1,0:T(8,128)(2,1)S(1)} collective-permute-done((bf16[64,2176]{1,0:T(8,128)(2,1)S(1)}, bf16[64,2176]{1,0:T(8,128)(2,1)S(1)}, u32[]{:S(2)}, u32[]{:S(2)}) %collective-permute-start.10) | collective-permute-done | bytes 278560 | tf_op jit(solution)/shard_map/ppermute | solution.py:175
  148.0 2.9 gather_fusion.1
  153.0 3.4 convolution_convert_fusion.2
  156.4 4.7 %all-to-all-start.2 = ((bf16[4,144,2048]{2,1,0:T(8,128)(2,1)}), bf16[4,144,2048]{2,1,0:T(8,128)(2,1)}, u32[]{:S(2)}, u32[]{:S(2)}) async-start(bf16[4,144,2048]{2,1,0:T(8,128)(2,1)} %bitcast.133), calls=%async_computation.5 | async-start | bytes 4718592 | tf_op jit(solution)/shard_map/all_to_all | solution.py:211
  161.1 3.3 pad_maximum_fusion
  166.7 23.0 %all-to-all-done.2 = bf16[4,144,2048]{2,1,0:T(8,128)(2,1)} async-done(((bf16[4,144,2048]{2,1,0:T(8,128)(2,1)}), bf16[4,144,2048]{2,1,0:T(8,128)(2,1)}, u32[]{:S(2)}, u32[]{:S(2)}) %all-to-all-start.2) | async-done | bytes 2359328 | tf_op jit(solution)/shard_map/all_to_all | solution.py:211
  189.7 4.6 %all-to-all-start = ((bf16[4,144,2048]{2,1,0:T(8,128)(2,1)}), bf16[4,144,2048]{2,1,0:T(8,128)(2,1)}, u32[]{:S(2)}, u32[]{:S(2)}) async-start(bf16[4,144,2048]{2,1,0:T(8,128)(2,1)} %bitcast.132), calls=%async_computation.2 | async-start | bytes 4718592 | tf_op jit(solution)/shard_map/all_to_all | solution.py:211
  194.8 5.8 %fusion.19 = f32[576,768]{1,0:T(8,128)} fusion(bf16[576,2048]{1,0:T(8,128)(2,1)} %bitcast.37, bf16[1,2048,384]{2,1,0:T(8,128)(2,1)} %collective-permute-done.4, bf16[1,2048,384]{2,1,0:T(8,128)(2,1)} %param.25), kind=kOutput, calls=%fused_computation.39 | convolution fusion | flops 1818230784 | bytes 7274496 | tf_op jit(solution)/shard_map/dot_general | solution.py:55
  200.5 22.3 %all-to-all-done = bf16[4,144,2048]{2,1,0:T(8,128)(2,1)} async-done(((bf16[4,144,2048]{2,1,0:T(8,128)(2,1)}), bf16[4,144,2048]{2,1,0:T(8,128)(2,1)}, u32[]{:S(2)}, u32[]{:S(2)}) %all-to-all-start) | async-done | bytes 2359328 | tf_op jit(solution)/shard_map/all_to_all | solution.py:211
  222.9 12.9 %collective-permute-done.8 = bf16[1,2048,768]{2,1,0:T(8,128)(2,1)} collective-permute-done((bf16[1,2048,768]{2,1,0:T(8,128)(2,1)}, bf16[1,2048,768]{2,1,0:T(8,128)(2,1)}, u32[]{:S(2)}, u32[]{:S(2)}) %collective-permute-start.8) | collective-permute-done | bytes 3145760 | tf_op jit(solution)/shard_map/ppermute | solution.py:48
  235.7 5.1 %fusion.84 = (bf16[1,2048,384]{2,1,0:T(8,128)(2,1)S(1)}, bf16[1,2048,384]{2,1,0:T(8,128)(2,1)}, bf16[1,2048,384]{2,1,0:T(8,128)(2,1)}, bf16[1,2048,384]{2,1,0:T(8,128)(2,1)}) fusion(bf16[1,2048,768]{2,1,0:T(8,128)(2,1)} %pad_maximum_fusion, bf16[1,2048,768]{2,1,0:T(8,128)(2,1)} %collective-permute-done.8), kind=kLoop, calls=%fused_computation.169 | loop fusion | bytes 12582912 | tf_op jit(solution)/shard_map/slice | solution.py:217
  240.8 9.4 %convolution_convert_fusion = bf16[576,2048]{1,0:T(8,128)(2,1)} fusion(bf16[1,2048,384]{2,1,0:T(8,128)(2,1)} %get-tuple-element.58, bf16[1,2048,384]{2,1,0:T(8,128)(2,1)} %get-tuple-element.50, f32[576,768]{1,0:T(8,128)} %fusion.19, bf16[576,2048]{1,0:T(8,128)(2,1)} %bitcast.37, bf16[1,2048,384]{2,1,0:T(8,128)(2,1)} %get-tuple-element.59, ...), kind=kOutput, calls=%fused_computation.19 | convolution fusion | flops 3640295424 | bytes 12779520 | tf_op jit(solution)/shard_map/rf,df->rd/dot_general | solution.py:58
  250.3 4.7 %all-to-all-start.3 = ((bf16[4,144,2048]{2,1,0:T(8,128)(2,1)}), bf16[4,144,2048]{2,1,0:T(8,128)(2,1)}, u32[]{:S(2)}, u32[]{:S(2)}) async-start(bf16[4,144,2048]{2,1,0:T(8,128)(2,1)} %bitcast.147), calls=%async_computation.6 | async-start | bytes 4718592 | tf_op jit(solution)/shard_map/all_to_all | solution.py:220
  256.4 5.8 %fusion.20 = f32[576,768]{1,0:T(8,128)} fusion(bf16[576,2048]{1,0:T(8,128)(2,1)} %bitcast.22, bf16[1,2048,384]{2,1,0:T(8,128)(2,1)} %collective-permute-done.4, bf16[1,2048,384]{2,1,0:T(8,128)(2,1)} %param.25), kind=kOutput, calls=%fused_computation.40 | convolution fusion | flops 1818230784 | bytes 7274496 | tf_op jit(solution)/shard_map/dot_general | solution.py:55
  262.3 9.4 %convolution_convert_fusion.1 = bf16[576,2048]{1,0:T(8,128)(2,1)} fusion(bf16[1,2048,384]{2,1,0:T(8,128)(2,1)} %get-tuple-element.58, bf16[1,2048,384]{2,1,0:T(8,128)(2,1)} %get-tuple-element.50, f32[576,768]{1,0:T(8,128)} %fusion.20, bf16[576,2048]{1,0:T(8,128)(2,1)} %bitcast.22, bf16[1,2048,384]{2,1,0:T(8,128)(2,1)} %get-tuple-element.59, ...), kind=kOutput, calls=%fused_computation.20 | convolution fusion | flops 3640295424 | bytes 12779520 | tf_op jit(solution)/shard_map/rf,df->rd/dot_general | solution.py:58
  271.7 11.7 %all-to-all-done.3 = bf16[4,144,2048]{2,1,0:T(8,128)(2,1)} async-done(((bf16[4,144,2048]{2,1,0:T(8,128)(2,1)}), bf16[4,144,2048]{2,1,0:T(8,128)(2,1)}, u32[]{:S(2)}, u32[]{:S(2)}) %all-to-all-start.3) | async-done | bytes 2359328 | tf_op jit(solution)/shard_map/all_to_all | solution.py:220
  283.3 4.5 %all-to-all-start.1 = ((bf16[4,144,2048]{2,1,0:T(8,128)(2,1)}), bf16[4,144,2048]{2,1,0:T(8,128)(2,1)}, u32[]{:S(2)}, u32[]{:S(2)}) async-start(bf16[4,144,2048]{2,1,0:T(8,128)(2,1)} %bitcast.146), calls=%async_computation.3 | async-start | bytes 4718592 | tf_op jit(solution)/shard_map/all_to_all | solution.py:220
  287.9 2.9 fusion.42
  290.8 3.6 %fusion.10 = bf16[256,2048]{1,0:T(8,128)(2,1)} fusion(f32[256,2048]{1,0:T(8,128)S(1)} %fusion.42, bf16[576,2048]{1,0:T(8,128)(2,1)} %bitcast.39, f32[576,256]{1,0:T(8,128)S(1)} %copy-done.3), kind=kOutput, calls=%fused_computation.26 | convolution fusion | flops 605618176 | bytes 6094848 | tf_op jit(solution)/shard_map/dot_general | solution.py:227
  296.9 19.5 %all-to-all-done.1 = bf16[4,144,2048]{2,1,0:T(8,128)(2,1)} async-done(((bf16[4,144,2048]{2,1,0:T(8,128)(2,1)}), bf16[4,144,2048]{2,1,0:T(8,128)(2,1)}, u32[]{:S(2)}, u32[]{:S(2)}) %all-to-all-start.1) | async-done | bytes 2359328 | tf_op jit(solution)/shard_map/all_to_all | solution.py:220
  316.4 2.7 fusion.45
  319.1 4.2 %fusion.9 = bf16[256,2048]{1,0:T(8,128)(2,1)} fusion(f32[256,2048]{1,0:T(8,128)S(1)} %fusion.45, bf16[576,2048]{1,0:T(8,128)(2,1)} %bitcast.27, f32[576,256]{1,0:T(8,128)} %copy-done.4), kind=kOutput, calls=%fused_computation.25 | convolution fusion | flops 605618176 | bytes 6094848 | tf_op jit(solution)/shard_map/dot_general | solution.py:227
  323.3 25.4 %reduce-scatter.9.cloned.1.call-done = bf16[1,64,2048]{2,1,0:T(8,128)(2,1)} async-done(((bf16[4,64,2048]{2,1,0:T(8,128)(2,1)}), bf16[1,64,2048]{2,1,0:T(8,128)(2,1)}) %reduce-scatter.9.cloned.1.call-update) | async-done | bytes 262160 | tf_op jit(solution)/shard_map/reduce_scatter | solution.py:229
  (128 shorter events, 53.2 us)
Async XLA Ops:
  6.5 18.7 %copy-start = (bf16[1024,1024]{1,0:T(8,128)(2,1)S(1)}, bf16[1024,1024]{1,0:T(8,128)(2,1)}, u32[]{:S(2)}) copy-start(bf16[1024,1024]{1,0:T(8,128)(2,1)} %param.20) | copy-start | bytes 6291460
  6.5 46.9 %reduce-scatter.5.cloned.1.call-start = ((), (), s32[]{:S(2)}) async-start(), calls=%async_computation.8 | async-start | bytes 1310720 | tf_op jit(solution)/shard_map/reduce_scatter | solution.py:129
  6.5 11.9 %collective-permute-start.1 = (s32[2,256]{1,0:T(2,128)}, s32[2,256]{1,0:T(2,128)S(1)}, u32[]{:S(2)}, u32[]{:S(2)}) collective-permute-start(s32[2,256]{1,0:T(2,128)} %param.17), channel_id=1, source_target_pairs={{0,16},{16,0},{1,17},{17,1},{2,18},{18,2},{3,19},{19,3},{4,20},{20... | collective-permute-start | bytes 6152 | tf_op jit(solution)/shard_map/ppermute | solution.py:48
  12.6 7.8 %collective-permute-start = (bf16[2,256,256]{2,1,0:T(8,128)(2,1)S(1)}, bf16[2,256,256]{2,1,0:T(8,128)(2,1)S(1)}, u32[]{:S(2)}, u32[]{:S(2)}) collective-permute-start(bf16[2,256,256]{2,1,0:T(8,128)(2,1)S(1)} %pad_maximum_fusion.4), channel_id=1, source_target_pairs={{0,16},{16,0},{1,17},{17,1},{2,18},{18,2},{3,19},{19,3},{4,20},{20... | collective-permute-start | bytes 786440 | tf_op jit(solution)/shard_map/ppermute | solution.py:48
  16.2 2.2 copy-start.12
  16.3 4.1 %copy-start.9 = (bf16[2,256,128]{2,1,0:T(8,128)(2,1)S(1)}, bf16[2,256,128]{2,1,0:T(8,128)(2,1)}, u32[]{:S(2)}) copy-start(bf16[2,256,128]{2,1,0:T(8,128)(2,1)} %param.16) | copy-start | bytes 393220
  27.6 53.8 %reduce-scatter.7.cloned.1.call-start = ((), (), s32[]{:S(2)}) async-start(), calls=%async_computation.9 | async-start | bytes 1310720 | tf_op jit(solution)/shard_map/reduce_scatter | solution.py:129
  29.6 27.2 %copy-start.13 = (s32[2,256,8]{1,2,0:T(8,128)S(1)}, s32[2,256,8]{1,2,0:T(8,128)}, u32[]{:S(2)}) copy-start(s32[2,256,8]{1,2,0:T(8,128)} %param.24) | copy-start | bytes 49156
  29.7 23.8 %collective-permute-start.2 = (bf16[512,1024]{1,0:T(8,128)(2,1)S(1)}, bf16[512,1024]{1,0:T(8,128)(2,1)S(1)}, u32[]{:S(2)}, u32[]{:S(2)}) collective-permute-start(bf16[512,1024]{1,0:T(8,128)(2,1)S(1)} %bitcast.151), channel_id=1, source_target_pairs={{0,16},{16,0},{1,17},{17,1},{2,18},{18,2},{3,19},{19,3},{4,20},{20... | collective-permute-start | bytes 3145736 | tf_op jit(solution)/shard_map/ppermute | solution.py:48
  53.4 43.9 %copy-start.10 = (bf16[2,64,1024]{2,1,0:T(8,128)(2,1)S(1)}, bf16[2,64,1024]{2,1,0:T(8,128)(2,1)}, u32[]{:S(2)}) copy-start(bf16[2,64,1024]{2,1,0:T(8,128)(2,1)} %reduce-scatter.5.cloned.1.call-done) | copy-start | bytes 786436
  55.7 43.6 %collective-permute-start.4 = (bf16[1,2048,384]{2,1,0:T(8,128)(2,1)}, bf16[1,2048,384]{2,1,0:T(8,128)(2,1)}, u32[]{:S(2)}, u32[]{:S(2)}) collective-permute-start(bf16[1,2048,384]{2,1,0:T(8,128)(2,1)} %param.25), channel_id=1, source_target_pairs={{0,16},{16,0},{1,17},{17,1},{2,18},{18,2},{3,19},{19,3},{4,20},{20... | collective-permute-start | bytes 4718600 | tf_op jit(solution)/shard_map/ppermute | solution.py:48
  81.4 15.9 %collective-permute-start.3 = (bf16[2,64,1024]{2,1,0:T(8,128)(2,1)}, bf16[2,64,1024]{2,1,0:T(8,128)(2,1)S(1)}, u32[]{:S(2)}, u32[]{:S(2)}) collective-permute-start(bf16[2,64,1024]{2,1,0:T(8,128)(2,1)} %reduce-scatter.7.cloned.1.call-done), channel_id=1, source_target_pairs={{0,16},{16,0},{1,17},{17,1},{2,18},{18,2},{3,19},{19,3},{4,20},{20... | collective-permute-start | bytes 786440 | tf_op jit(solution)/shard_map/ppermute | solution.py:131
  99.5 11.4 %collective-permute-start.5 = (bf16[64,2176]{1,0:T(8,128)(2,1)S(1)}, bf16[64,2176]{1,0:T(8,128)(2,1)S(1)}, u32[]{:S(2)}, u32[]{:S(2)}) collective-permute-start(bf16[64,2176]{1,0:T(8,128)(2,1)S(1)} %get-tuple-element.55), channel_id=1, source_target_pairs={{0,1},{1,2},{2,3},{3,0},{4,5},{5,6},{6,7},{7,4},{8,9},{9,10},{10,1... | collective-permute-start | bytes 835592 | tf_op jit(solution)/shard_map/ppermute | solution.py:175
  101.0 14.4 %collective-permute-start.7 = (bf16[64,2176]{1,0:T(8,128)(2,1)S(1)}, bf16[64,2176]{1,0:T(8,128)(2,1)S(1)}, u32[]{:S(2)}, u32[]{:S(2)}) collective-permute-start(bf16[64,2176]{1,0:T(8,128)(2,1)S(1)} %get-tuple-element.55), channel_id=1, source_target_pairs={{1,0},{2,1},{3,2},{0,3},{5,4},{6,5},{7,6},{4,7},{9,8},{10,9},{11,1... | collective-permute-start | bytes 835592 | tf_op jit(solution)/shard_map/ppermute | solution.py:177
  110.9 9.4 %collective-permute-start.6 = (bf16[64,2176]{1,0:T(8,128)(2,1)S(1)}, bf16[64,2176]{1,0:T(8,128)(2,1)S(1)}, u32[]{:S(2)}, u32[]{:S(2)}) collective-permute-start(bf16[64,2176]{1,0:T(8,128)(2,1)S(1)} %collective-permute-done.5), channel_id=1, source_target_pairs={{0,1},{1,2},{2,3},{3,0},{4,5},{5,6},{6,7},{7,4},{8,9},{9,10},{10,1... | collective-permute-start | bytes 835592 | tf_op jit(solution)/shard_map/ppermute | solution.py:175
  123.4 24.6 %copy-start.5 = (bf16[4,64,2176]{2,1,0:T(8,128)(2,1)}, bf16[4,64,2176]{2,1,0:T(8,128)(2,1)S(1)}, u32[]{:S(2)}) copy-start(bf16[4,64,2176]{2,1,0:T(8,128)(2,1)S(1)} %gather_fusion) | copy-start | bytes 3342340
  126.9 11.5 %collective-permute-start.9 = (bf16[64,2176]{1,0:T(8,128)(2,1)S(1)}, bf16[64,2176]{1,0:T(8,128)(2,1)S(1)}, u32[]{:S(2)}, u32[]{:S(2)}) collective-permute-start(bf16[64,2176]{1,0:T(8,128)(2,1)S(1)} %get-tuple-element.34), channel_id=1, source_target_pairs={{0,1},{1,2},{2,3},{3,0},{4,5},{5,6},{6,7},{7,4},{8,9},{9,10},{10,1... | collective-permute-start | bytes 835592 | tf_op jit(solution)/shard_map/ppermute | solution.py:175
  126.9 13.7 %collective-permute-start.11 = (bf16[64,2176]{1,0:T(8,128)(2,1)S(1)}, bf16[64,2176]{1,0:T(8,128)(2,1)S(1)}, u32[]{:S(2)}, u32[]{:S(2)}) collective-permute-start(bf16[64,2176]{1,0:T(8,128)(2,1)S(1)} %get-tuple-element.34), channel_id=1, source_target_pairs={{1,0},{2,1},{3,2},{0,3},{5,4},{6,5},{7,6},{4,7},{9,8},{10,9},{11,1... | collective-permute-start | bytes 835592 | tf_op jit(solution)/shard_map/ppermute | solution.py:177
  138.4 8.4 %collective-permute-start.10 = (bf16[64,2176]{1,0:T(8,128)(2,1)S(1)}, bf16[64,2176]{1,0:T(8,128)(2,1)S(1)}, u32[]{:S(2)}, u32[]{:S(2)}) collective-permute-start(bf16[64,2176]{1,0:T(8,128)(2,1)S(1)} %collective-permute-done.9), channel_id=1, source_target_pairs={{0,1},{1,2},{2,3},{3,0},{4,5},{5,6},{6,7},{7,4},{8,9},{9,10},{10,1... | collective-permute-start | bytes 835592 | tf_op jit(solution)/shard_map/ppermute | solution.py:175
  156.4 4.7 %copy-start.8 = (bf16[1,2048,384]{2,1,0:T(8,128)(2,1)S(1)}, bf16[1,2048,384]{2,1,0:T(8,128)(2,1)}, u32[]{:S(2)}) copy-start(bf16[1,2048,384]{2,1,0:T(8,128)(2,1)} %param.27) | copy-start | bytes 4718596
  156.4 33.2 %all-to-all-start.2 = ((bf16[4,144,2048]{2,1,0:T(8,128)(2,1)}), bf16[4,144,2048]{2,1,0:T(8,128)(2,1)}, u32[]{:S(2)}, u32[]{:S(2)}) async-start(bf16[4,144,2048]{2,1,0:T(8,128)(2,1)} %bitcast.133), calls=%async_computation.5 | async-start | bytes 4718592 | tf_op jit(solution)/shard_map/all_to_all | solution.py:211
  164.4 71.3 %collective-permute-start.8 = (bf16[1,2048,768]{2,1,0:T(8,128)(2,1)}, bf16[1,2048,768]{2,1,0:T(8,128)(2,1)}, u32[]{:S(2)}, u32[]{:S(2)}) collective-permute-start(bf16[1,2048,768]{2,1,0:T(8,128)(2,1)} %pad_maximum_fusion), channel_id=1, source_target_pairs={{0,16},{16,0},{1,17},{17,1},{2,18},{18,2},{3,19},{19,3},{4,20},{20... | collective-permute-start | bytes 9437192 | tf_op jit(solution)/shard_map/ppermute | solution.py:48
  189.7 4.7 %copy-start.6 = (bf16[4,64,2176]{2,1,0:T(8,128)(2,1)S(1)}, bf16[4,64,2176]{2,1,0:T(8,128)(2,1)}, u32[]{:S(2)}) copy-start(bf16[4,64,2176]{2,1,0:T(8,128)(2,1)} %gather_fusion.1) | copy-start | bytes 3342340
  189.7 4.7 %copy-start.15 = (bf16[2048,16]{0,1:T(8,128)(2,1)S(1)}, bf16[2048,16]{0,1:T(8,128)(2,1)}, u32[]{:S(2)}) copy-start(bf16[2048,16]{0,1:T(8,128)(2,1)} %param.23) | copy-start | bytes 196612
  189.7 33.2 %all-to-all-start = ((bf16[4,144,2048]{2,1,0:T(8,128)(2,1)}), bf16[4,144,2048]{2,1,0:T(8,128)(2,1)}, u32[]{:S(2)}, u32[]{:S(2)}) async-start(bf16[4,144,2048]{2,1,0:T(8,128)(2,1)} %bitcast.132), calls=%async_computation.2 | async-start | bytes 4718592 | tf_op jit(solution)/shard_map/all_to_all | solution.py:211
  250.3 33.1 %all-to-all-start.3 = ((bf16[4,144,2048]{2,1,0:T(8,128)(2,1)}), bf16[4,144,2048]{2,1,0:T(8,128)(2,1)}, u32[]{:S(2)}, u32[]{:S(2)}) async-start(bf16[4,144,2048]{2,1,0:T(8,128)(2,1)} %bitcast.147), calls=%async_computation.6 | async-start | bytes 4718592 | tf_op jit(solution)/shard_map/all_to_all | solution.py:220
  283.3 33.1 %all-to-all-start.1 = ((bf16[4,144,2048]{2,1,0:T(8,128)(2,1)}), bf16[4,144,2048]{2,1,0:T(8,128)(2,1)}, u32[]{:S(2)}, u32[]{:S(2)}) async-start(bf16[4,144,2048]{2,1,0:T(8,128)(2,1)} %bitcast.146), calls=%async_computation.3 | async-start | bytes 4718592 | tf_op jit(solution)/shard_map/all_to_all | solution.py:220
  287.8 35.5 %reduce-scatter.11.cloned.1.call-start = ((), (), s32[]{:S(2)}) async-start(), calls=%async_computation.11 | async-start | bytes 1310720 | tf_op jit(solution)/shard_map/reduce_scatter | solution.py:229
  287.9 2.9 copy-start.3
  294.5 54.3 %reduce-scatter.9.cloned.1.call-start = ((), (), s32[]{:S(2)}) async-start(), calls=%async_computation.10 | async-start | bytes 1310720 | tf_op jit(solution)/shard_map/reduce_scatter | solution.py:229
  296.9 19.6 %copy-start.4 = (f32[576,256]{1,0:T(8,128)}, f32[576,256]{1,0:T(8,128)S(1)}, u32[]{:S(2)}) copy-start(f32[576,256]{1,0:T(8,128)S(1)} %select_reduce_fusion.1) | copy-start | bytes 1769476
  319.1 31.6 %copy-start.1 = (bf16[1024,1024]{1,0:T(8,128)(2,1)S(1)}, bf16[1024,1024]{1,0:T(8,128)(2,1)}, u32[]{:S(2)}) copy-start(bf16[1024,1024]{1,0:T(8,128)(2,1)} %param.20) | copy-start | bytes 6291460
  (4 other events, 6.1 us)
Sparse Core Ops, SparseCore 0:
  27.7 25.2 reduce-scatter.4
  55.8 25.4 reduce-scatter.6
  294.6 26.0 reduce-scatter.10
  323.4 25.2 reduce-scatter.8
